TPU v7x, 128 devices: a whole 4x4x4 slice. The times are simulated.
128 devices in a mesh: fsdp: 32 (over y, z, core), seq: 4 (over x).
Axes of the slice: x: 4, y: 4, z: 4, core: 2. Of those that a mesh axis runs over, the one named last changes fastest.
Arguments:
- draft_tokens: bfloat16 [32768, 2048], P('fsdp'), may hold values from -6 to 6
- draft_gate: bfloat16 [2048, 4096], P('fsdp', 'seq'), may hold values from -0.125 to 0.125
- draft_up: bfloat16 [2048, 4096], P('fsdp', 'seq'), may hold values from -0.125 to 0.125
- draft_head: float32 [4096], P('seq'), may hold values from -0.75 to 0.75
- verifier_rows: bfloat16 [32768, 8192], P(('fsdp', 'seq')), may hold values from -6 to 6
- norm_gain: float32 [8192], replicated, may hold values from 0.5 to 1.5
- key_weight: bfloat16 [8192, 512], P('fsdp'), may hold values from -0.06629126 to 0.06629126
- value_weight: bfloat16 [8192, 512], P('fsdp'), may hold values from -0.0625 to 0.0625
- pool_query: float32 [4, 4, 128], replicated, may hold values from -32 to 32
- flags: int32 [1024], P(('fsdp', 'seq')), may hold values from 0 to 1, as said below
- owner: int32 [1024], P(('fsdp', 'seq')), may hold values from 0 to 3
Outputs:
- draft_score: float32 [1024], P(('fsdp', 'seq'))
- verdict: bfloat16 [1024, 512], P(('fsdp', 'seq'))
Inputs may be any that keep to these rules, and one draw needn't show every extreme that they name: `flags`: on the 8 segments of one device, at most 4 flagged segments share an owner lane, and on every device exactly 4 flagged segments share one lane.
All inputs are finite; a program needn't handle non-finite values.
Results may differ from a plain program's by a relative error of at most 0.009.
Values may be sent and summed in bfloat16 or wider, within the bound.
No kernel may reach another device: no remote copies, remote signals or barrier semaphores. Data moves between devices by JAX's collectives and lax.ppermute only.
A program may use at most 128 MiB of HBM per device.

v0:
```python
import math
import jax
import jax.numpy as jnp
from jax import lax
from jax.sharding import PartitionSpec as P

KVH = 4
HD = 128
SEGL = 32
eps = 1e-05


def normalize_rows(rows, norm_gain):
    values = rows.astype(jnp.float32)
    scale = lax.rsqrt(jnp.mean(values * values, axis=-1, keepdims=True) + eps)
    return (values * scale * norm_gain).astype(jnp.bfloat16)


def segment_pool(seg_keys, seg_values, queries, head_size):
    scores = jnp.einsum(
        "sthd,shd->sth", seg_keys, queries, precision=lax.Precision.HIGHEST
    ) / math.sqrt(head_size)
    scores = scores - jnp.max(scores, axis=1, keepdims=True)
    weights = jnp.exp(scores)
    weights = weights / jnp.sum(weights, axis=1, keepdims=True)
    summary_key = jnp.einsum("sth,sthd->shd", weights, seg_keys, precision=lax.Precision.HIGHEST)
    summary_value = jnp.einsum(
        "sth,sthd->shd", weights, seg_values, precision=lax.Precision.HIGHEST
    )
    return (summary_key, summary_value)


def cross_pool(query_keys, key_all, value_all, live_all, head_size):
    scores = jnp.einsum(
        "jhd,ihd->jhi", query_keys, key_all, precision=lax.Precision.HIGHEST
    ) / math.sqrt(head_size)
    scores = jnp.where(live_all[None, None, :], scores, -1e30)
    highest = jnp.max(scores, axis=2, keepdims=True)
    weights = jnp.where(live_all[None, None, :], jnp.exp(scores - highest), 0.0)
    total = jnp.sum(weights, axis=2, keepdims=True)
    return jnp.einsum("jhi,ihd->jhd", weights, value_all, precision=lax.Precision.HIGHEST) / total


def project_pair(row_block, pieces):
    return (
        jnp.dot(row_block, pieces[0], preferred_element_type=jnp.float32),
        jnp.dot(row_block, pieces[1], preferred_element_type=jnp.float32),
    )


def local(
    draft_tokens,
    draft_gate,
    draft_up,
    draft_head,
    verifier_rows,
    norm_gain,
    key_weight,
    value_weight,
    pool_query,
    flags,
    owner,
):
    seg_count = flags.shape[0]
    gate, upward = project_pair(
        draft_tokens,
        (
            lax.all_gather(draft_gate, "fsdp", axis=0, tiled=True),
            lax.all_gather(draft_up, "fsdp", axis=0, tiled=True),
        ),
    )
    partial_scores = jnp.sum(jax.nn.silu(gate) * upward * draft_head[None, :], axis=1)
    own_scores = lax.psum_scatter(partial_scores, "seq", scatter_dimension=0, tiled=True)
    draft_score = jnp.mean(own_scores.reshape(seg_count, SEGL), axis=1)
    normed = normalize_rows(verifier_rows, norm_gain)
    seg_keys, seg_values = project_pair(
        normed,
        (
            lax.all_gather(key_weight, "fsdp", axis=0, tiled=True),
            lax.all_gather(value_weight, "fsdp", axis=0, tiled=True),
        ),
    )
    lane_pick = (
        owner[:, None] == jnp.arange(pool_query.shape[0], dtype=jnp.int32)[None, :]
    ).astype(jnp.float32)
    queries = jnp.einsum("sc,chd->shd", lane_pick, pool_query, precision=lax.Precision.HIGHEST)
    summary_key, summary_value = segment_pool(
        seg_keys.reshape(seg_count, SEGL, KVH, HD),
        seg_values.reshape(seg_count, SEGL, KVH, HD),
        queries,
        HD,
    )
    live_own = flags.astype(jnp.float32)
    key_all, value_all, live_all = (
        lax.all_gather(summary_key.reshape(seg_count, KVH * HD), "seq", axis=0, tiled=True),
        lax.all_gather(summary_value.reshape(seg_count, KVH * HD), "seq", axis=0, tiled=True),
        lax.all_gather(live_own, "seq", axis=0, tiled=True),
    )
    pooled = cross_pool(
        summary_key,
        key_all.reshape(-1, KVH, HD),
        value_all.reshape(-1, KVH, HD),
        live_all > 0.5,
        HD,
    )
    own_pooled = pooled.reshape(seg_count, KVH * HD)
    verdict = jnp.where(
        flags[:, None] == 1, jax.nn.sigmoid(draft_score)[:, None] * own_pooled, 0.0
    ).astype(jnp.bfloat16)
    return (draft_score, verdict)


def solution(mesh):
    return jax.shard_map(
        local,
        mesh=mesh,
        in_specs=(
            P("fsdp", None),
            P("fsdp", "seq"),
            P("fsdp", "seq"),
            P("seq"),
            P(("fsdp", "seq"), None),
            P(),
            P("fsdp", None),
            P("fsdp", None),
            P(),
            P(("fsdp", "seq")),
            P(("fsdp", "seq")),
        ),
        out_specs=(P(("fsdp", "seq")), P(("fsdp", "seq"), None)),
        check_vma=False,
    )
```

profile of v0, /device:TPU:0, one launch (start us, length us, event | category | flops | bytes accessed | tf_op | source)
XLA Modules:
  0.0 243.5 jit_solution(6076633560900266448)
XLA Ops:
  7.2 0.7 all-gather.5.cloned.1.call-update
  8.0 0.7 all-gather.7.cloned.1.call-update
  8.7 0.7 all-gather.9.cloned.1.call-update
  10.0 1.3 fusion.44
  12.6 0.9 convolution_bitcast_fusion.1
  13.5 0.7 broadcast_compare_fusion.1
  14.1 0.7 convert_dynamic-update-slice_fusion
  14.9 3.1 %fusion.1 = f32[256]{0:T(256)S(1)} fusion(bf16[256,8192]{1,0:T(8,128)(2,1)} %param.15), kind=kLoop, calls=%fused_computation.3 | loop fusion | flops 6291200 | bytes 4195328 | tf_op jit(solution)/shard_map/reduce_sum | solution.py:15
  18.0 41.0 %all-gather.5.cloned.1.call-done = bf16[2048,1024]{1,0:T(8,128)(2,1)} async-done(((bf16[64,1024]{1,0:T(8,128)(2,1)}), bf16[2048,1024]{1,0:T(8,128)(2,1)}) %all-gather.5.cloned.1.call-update) | async-done | bytes 4194320 | tf_op jit(solution)/shard_map/all_gather | solution.py:68
  59.0 10.0 %fusion.47 = f32[1024,1024]{0,1:T(8,128)} fusion(bf16[1024,2048]{1,0:T(8,128)(2,1)} %param.11, bf16[2048,1024]{1,0:T(8,128)(2,1)} %all-gather.5.cloned.1.call-done), kind=kOutput, calls=%fused_computation.63 | convolution fusion | flops 4294967296 | bytes 12582912 | tf_op jit(solution)/shard_map/dot_general | solution.py:46
  69.0 37.8 %all-gather.7.cloned.1.call-done = bf16[2048,1024]{1,0:T(8,128)(2,1)} async-done(((bf16[64,1024]{1,0:T(8,128)(2,1)}), bf16[2048,1024]{1,0:T(8,128)(2,1)}) %all-gather.7.cloned.1.call-update) | async-done | bytes 4194320 | tf_op jit(solution)/shard_map/all_gather | solution.py:69
  106.7 10.1 %multiply_reduce_fusion = f32[1024]{0:T(1024)S(1)} fusion(f32[1024,1024]{0,1:T(8,128)} %fusion.47, bf16[1024,2048]{1,0:T(8,128)(2,1)} %param.11, bf16[2048,1024]{1,0:T(8,128)(2,1)} %all-gather.7.cloned.1.call-done, f32[1024]{0:T(1024)S(1)} %copy-done.2), kind=kOutput, calls=%fused_computation.6 | convolution fusion | flops 4302306304 | bytes 12591104 | tf_op jit(solution)/shard_map/dot_general | solution.py:47
  116.9 10.7 %all-reduce.2 = (f32[1024]{0:T(1024)S(1)}, f32[32]{0:T(128)S(1)}) all-reduce(f32[1024]{0:T(1024)S(1)} %multiply_reduce_fusion, f32[32]{0:T(128)S(1)} %convert_dynamic-update-slice_fusion), channel_id=2, replica_groups=mesh['fsdp'=32,'seq'=4] {'seq'}, use_global_device_ids=true, to_apply=%region_1.2.clone | all-reduce | flops 1056 | bytes 8448
  128.4 32.8 %all-gather.9.cloned.1.call-done = bf16[8192,512]{1,0:T(8,128)(2,1)} async-done(((bf16[256,512]{1,0:T(8,128)(2,1)}), bf16[8192,512]{1,0:T(8,128)(2,1)}) %all-gather.9.cloned.1.call-update) | async-done | bytes 8388624 | tf_op jit(solution)/shard_map/all_gather | solution.py:79
  161.2 7.0 %fusion.6 = f32[256,512]{1,0:T(8,128)S(1)} fusion(bf16[8192,512]{1,0:T(8,128)(2,1)} %all-gather.9.cloned.1.call-done, bf16[256,8192]{1,0:T(8,128)(2,1)} %param.15, f32[8192]{0:T(1024)S(1)} %copy-done.1, f32[256]{0:T(256)S(1)} %add_rsqrt_fusion), kind=kOutput, calls=%fused_computation.8 | convolution fusion | flops 2155872256 | bytes 13140992 | tf_op jit(solution)/shard_map/dot_general | solution.py:46
  168.4 0.9 fusion.21
  169.3 0.7 fusion.45
  170.1 0.5 fusion.19
  170.6 12.2 %all_gather.27 = f32[32,512]{1,0:T(8,128)S(1)} all-gather(f32[8,512]{1,0:T(8,128)S(1)} %bitcast.83), channel_id=1, replica_groups=mesh['fsdp'=32,'seq'=4] {'seq'}, dimensions={0}, use_global_device_ids=true | all-gather | bytes 81920 | tf_op jit(solution)/shard_map/all_gather | solution.py:95
  182.8 32.9 %all-gather.11.cloned.1.call-done = bf16[8192,512]{1,0:T(8,128)(2,1)} async-done(((bf16[256,512]{1,0:T(8,128)(2,1)}), bf16[8192,512]{1,0:T(8,128)(2,1)}) %all-gather.11.cloned.1.call-update) | async-done | bytes 8388624 | tf_op jit(solution)/shard_map/all_gather | solution.py:80
  215.7 7.0 %fusion.4 = f32[256,512]{1,0:T(8,128)S(1)} fusion(bf16[8192,512]{1,0:T(8,128)(2,1)} %all-gather.11.cloned.1.call-done, bf16[256,8192]{1,0:T(8,128)(2,1)} %param.15, f32[8192]{0:T(1024)S(1)} %copy-done.1, f32[256]{0:T(256)S(1)} %add_rsqrt_fusion), kind=kOutput, calls=%fused_computation.7 | convolution fusion | flops 2155872256 | bytes 13140992 | tf_op jit(solution)/shard_map/dot_general | solution.py:47
  222.9 0.5 fusion.17
  223.5 12.2 %all_gather.25 = f32[32,512]{1,0:T(8,128)S(1)} all-gather(f32[8,512]{1,0:T(8,128)S(1)} %bitcast.82), channel_id=1, replica_groups=mesh['fsdp'=32,'seq'=4] {'seq'}, dimensions={0}, use_global_device_ids=true | all-gather | bytes 81920 | tf_op jit(solution)/shard_map/all_gather | solution.py:96
  236.1 0.9 fusion.16
  (25 shorter events, 2.4 us)
Async XLA Ops:
  7.2 5.4 %copy-start = (f32[4,4,128]{2,1,0:T(4,128)S(1)}, f32[4,4,128]{2,1,0:T(4,128)}, u32[]{:S(2)}) copy-start(f32[4,4,128]{2,1,0:T(4,128)} %param.19) | copy-start | bytes 24580
  7.2 51.8 %all-gather.5.cloned.1.call-start = ((), (), s32[]{:S(2)}) async-start(), calls=%async_computation | async-start | bytes 4325376 | tf_op jit(solution)/shard_map/all_gather | solution.py:68
  7.9 98.8 %all-gather.7.cloned.1.call-start = ((), (), s32[]{:S(2)}) async-start(), calls=%async_computation.1 | async-start | bytes 4325376 | tf_op jit(solution)/shard_map/all_gather | solution.py:69
  8.7 152.5 %all-gather.9.cloned.1.call-start = ((), (), s32[]{:S(2)}) async-start(), calls=%async_computation.2 | async-start | bytes 8650752 | tf_op jit(solution)/shard_map/all_gather | solution.py:79
  9.4 206.3 %all-gather.11.cloned.1.call-start = ((), (), s32[]{:S(2)}) async-start(), calls=%async_computation.3 | async-start | bytes 8650752 | tf_op jit(solution)/shard_map/all_gather | solution.py:80
  18.0 88.7 %copy-start.2 = (f32[1024]{0:T(1024)S(1)}, f32[1024]{0:T(1024)}, u32[]{:S(2)}) copy-start(f32[1024]{0:T(1024)} %param.14) | copy-start | bytes 12292
  69.0 92.2 %copy-start.1 = (f32[8192]{0:T(1024)S(1)}, f32[8192]{0:T(1024)}, u32[]{:S(2)}) copy-start(f32[8192]{0:T(1024)} %param.16) | copy-start | bytes 98308
Sparse Core Ops, SparseCore 0:
  10.2 48.6 all-gather.4
  61.2 45.4 all-gather.6
  109.0 52.1 all-gather.8
  163.3 52.3 all-gather.10
where the time goes:
time: 244 us; the launch traced here: 243 us
  waiting for transfers between devices  147 us (60%)
  matrix products  38.2 us (16%)
  blocking collectives  35 us (14%)
  between operations  15.2 us (6%)
  other arithmetic  6.1 us (2%)
    all_gather x1, waiting for transfers between devices, local(): lax.all_gather(draft_gate, 'fsdp', axis=0, tiled=True)  41 us
    all_gather x1, waiting for transfers between devices, local(): lax.all_gather(draft_up, 'fsdp', axis=0, tiled=True)  37.8 us
    all_gather x1, waiting for transfers between devices, local(): lax.all_gather(value_weight, 'fsdp', axis=0, tiled=True)  32.9 us
    all_gather x1, waiting for transfers between devices, local(): lax.all_gather(key_weight, 'fsdp', axis=0, tiled=True)  32.8 us
    dot_general x2, matrix products, project_pair(): jnp.dot(row_block, pieces[1], preferred_element_type=jnp.float32)  17.2 us
    dot_general x2, matrix products, project_pair(): jnp.dot(row_block, pieces[0], preferred_element_type=jnp.float32)  17 us
    all_gather x1, blocking collectives, local(): lax.all_gather(summary_value.reshape(seg_count, KVH * HD), 'seq', axis=0,...  12.2 us
    all_gather x1, blocking collectives, local(): lax.all_gather(summary_key.reshape(seg_count, KVH * HD), 'seq', axis=0, t...  12.2 us
  transfers between devices with their start and end apart: 4, of which 4 were waited for; matrix products, arithmetic and copies ran while one was open for 15% of the time, Pallas kernels for 0%

commit v1 on v0

--- a/solution.py
+++ b/solution.py
@@ -8,6 +8,22 @@
 HD = 128
 SEGL = 32
 eps = 1e-05
+
+
+def gather_around(x, axis, dim):
+    ways, here, lap = (lax.axis_size(axis), lax.axis_index(axis), x.shape[dim])
+    shape = [n * ways if d == dim else n for d, n in enumerate(x.shape)]
+    full = lax.dynamic_update_slice_in_dim(jnp.zeros(shape, x.dtype), x, here * lap, axis=dim)
+    going_up = going_down = x
+    for far in range(1, ways // 2 + 1):
+        going_up = lax.ppermute(going_up, axis, [(d, (d + 1) % ways) for d in range(ways)])
+        full = lax.dynamic_update_slice_in_dim(full, going_up, (here - far) % ways * lap, axis=dim)
+        if 2 * far < ways:
+            going_down = lax.ppermute(going_down, axis, [(d, (d - 1) % ways) for d in range(ways)])
+            full = lax.dynamic_update_slice_in_dim(
+                full, going_down, (here + far) % ways * lap, axis=dim
+            )
+    return full
 
 
 def normalize_rows(rows, norm_gain):
@@ -93,7 +109,7 @@
     live_own = flags.astype(jnp.float32)
     key_all, value_all, live_all = (
         lax.all_gather(summary_key.reshape(seg_count, KVH * HD), "seq", axis=0, tiled=True),
-        lax.all_gather(summary_value.reshape(seg_count, KVH * HD), "seq", axis=0, tiled=True),
+        gather_around(summary_value.reshape(seg_count, KVH * HD), "seq", 0),
         lax.all_gather(live_own, "seq", axis=0, tiled=True),
     )
     pooled = cross_pool(

time: 244 us -> 252 us (1.033)
  waiting for transfers between devices: 147 us -> 164 us
  blocking collectives: 35 us -> 22.6 us
  starting transfers between devices: 0.15 us -> 3.71 us
    all_gather x1, waiting for transfers between devices: 32.9 us -> 45.1 us  [local(): lax.all_gather(value_weight, 'fsdp', axis=0, tiled=True)]
    all_gather x1 -> x0, blocking collectives: 12.2 us -> none  [local(): lax.all_gather(summary_value.reshape(seg_count, KVH * HD), 'seq', axis=0,...]
    ppermute x0 -> x3, waiting for transfers between devices: none -> 4.75 us  [the longest x2 4.75 us: gather_around(): lax.ppermute(going_up, axis, [(d, (d + 1) % ways) for d in range(ways)])]
    ppermute x0 -> x3, starting transfers between devices: none -> 3.56 us  [the longest x1 1.78 us: gather_around(): lax.ppermute(going_down, axis, [(d, (d - 1) % ways) for d in range(ways)])]
  transfers between devices with their start and end apart: 4 -> 7, of which waited for: 4 -> 5; matrix products, arithmetic and copies ran while one was open for 15% -> 15% of each run, Pallas kernels for 0% -> 0%
where the time goes in v1:
time: 252 us
  waiting for transfers between devices  164 us (65%)
  matrix products  38.2 us (15%)
  blocking collectives  22.6 us (9%)
  between operations  15.2 us (6%)
  other arithmetic  6.07 us (2%)
  starting transfers between devices  3.71 us (1%)
    all_gather x1, waiting for transfers between devices, local(): lax.all_gather(value_weight, 'fsdp', axis=0, tiled=True)  45.1 us
    all_gather x1, waiting for transfers between devices, local(): lax.all_gather(draft_gate, 'fsdp', axis=0, tiled=True)  40.9 us
    all_gather x1, waiting for transfers between devices, local(): lax.all_gather(draft_up, 'fsdp', axis=0, tiled=True)  37.8 us
    all_gather x1, waiting for transfers between devices, local(): lax.all_gather(key_weight, 'fsdp', axis=0, tiled=True)  32.8 us
    dot_general x2, matrix products, project_pair(): jnp.dot(row_block, pieces[1], preferred_element_type=jnp.float32)  17.2 us
    dot_general x2, matrix products, project_pair(): jnp.dot(row_block, pieces[0], preferred_element_type=jnp.float32)  17 us
    all_gather x1, blocking collectives, local(): lax.all_gather(summary_key.reshape(seg_count, KVH * HD), 'seq', axis=0, t...  11.9 us
    unnamed x1, blocking collectives  10.7 us
  transfers between devices with their start and end apart: 7, of which 5 were waited for; matrix products, arithmetic and copies ran while one was open for 15% of the time, Pallas kernels for 0%

profile of v1, /device:TPU:0, one launch (start us, length us, event | category | flops | bytes accessed | tf_op | source)
XLA Modules:
  0.0 251.6 jit_solution(2723334123687598773)
XLA Ops:
  7.2 0.7 all-gather.5.cloned.1.call-update
  8.0 0.7 all-gather.7.cloned.1.call-update
  8.7 0.7 all-gather.9.cloned.1.call-update
  10.0 1.3 fusion.44
  12.7 0.9 convolution_bitcast_fusion.1
  13.5 0.7 broadcast_compare_fusion.1
  14.2 0.7 convert_dynamic-update-slice_fusion
  14.9 3.1 %fusion.1 = f32[256]{0:T(256)S(1)} fusion(bf16[256,8192]{1,0:T(8,128)(2,1)} %param.15), kind=kLoop, calls=%fused_computation.3 | loop fusion | flops 6291200 | bytes 4195328 | tf_op jit(solution)/shard_map/reduce_sum | solution.py:31
  18.1 40.9 %all-gather.5.cloned.1.call-done = bf16[2048,1024]{1,0:T(8,128)(2,1)} async-done(((bf16[64,1024]{1,0:T(8,128)(2,1)}), bf16[2048,1024]{1,0:T(8,128)(2,1)}) %all-gather.5.cloned.1.call-update) | async-done | bytes 4194320 | tf_op jit(solution)/shard_map/all_gather | solution.py:84
  59.0 10.0 %fusion.47 = f32[1024,1024]{0,1:T(8,128)} fusion(bf16[1024,2048]{1,0:T(8,128)(2,1)} %param.11, bf16[2048,1024]{1,0:T(8,128)(2,1)} %all-gather.5.cloned.1.call-done), kind=kOutput, calls=%fused_computation.67 | convolution fusion | flops 4294967296 | bytes 12582912 | tf_op jit(solution)/shard_map/dot_general | solution.py:62
  69.0 37.8 %all-gather.7.cloned.1.call-done = bf16[2048,1024]{1,0:T(8,128)(2,1)} async-done(((bf16[64,1024]{1,0:T(8,128)(2,1)}), bf16[2048,1024]{1,0:T(8,128)(2,1)}) %all-gather.7.cloned.1.call-update) | async-done | bytes 4194320 | tf_op jit(solution)/shard_map/all_gather | solution.py:85
  106.7 10.1 %multiply_reduce_fusion = f32[1024]{0:T(1024)S(1)} fusion(f32[1024,1024]{0,1:T(8,128)} %fusion.47, bf16[1024,2048]{1,0:T(8,128)(2,1)} %param.11, bf16[2048,1024]{1,0:T(8,128)(2,1)} %all-gather.7.cloned.1.call-done, f32[1024]{0:T(1024)S(1)} %copy-done.2), kind=kOutput, calls=%fused_computation.6 | convolution fusion | flops 4302306304 | bytes 12591104 | tf_op jit(solution)/shard_map/dot_general | solution.py:63
  116.9 10.7 %all-reduce.2 = (f32[1024]{0:T(1024)S(1)}, f32[32]{0:T(128)S(1)}) all-reduce(f32[1024]{0:T(1024)S(1)} %multiply_reduce_fusion, f32[32]{0:T(128)S(1)} %convert_dynamic-update-slice_fusion), channel_id=2, replica_groups=mesh['fsdp'=32,'seq'=4] {'seq'}, use_global_device_ids=true, to_apply=%region_1.2.clone | all-reduce | flops 1056 | bytes 8448
  128.4 32.8 %all-gather.9.cloned.1.call-done = bf16[8192,512]{1,0:T(8,128)(2,1)} async-done(((bf16[256,512]{1,0:T(8,128)(2,1)}), bf16[8192,512]{1,0:T(8,128)(2,1)}) %all-gather.9.cloned.1.call-update) | async-done | bytes 8388624 | tf_op jit(solution)/shard_map/all_gather | solution.py:95
  161.2 7.0 %fusion.6 = f32[256,512]{1,0:T(8,128)S(1)} fusion(bf16[8192,512]{1,0:T(8,128)(2,1)} %all-gather.9.cloned.1.call-done, bf16[256,8192]{1,0:T(8,128)(2,1)} %param.15, f32[8192]{0:T(1024)S(1)} %copy-done.1, f32[256]{0:T(256)S(1)} %add_rsqrt_fusion), kind=kOutput, calls=%fused_computation.8 | convolution fusion | flops 2155872256 | bytes 13140992 | tf_op jit(solution)/shard_map/dot_general | solution.py:62
  168.4 0.9 fusion.21
  169.3 0.7 fusion.45
  170.6 45.1 %all-gather.11.cloned.1.call-done = bf16[8192,512]{1,0:T(8,128)(2,1)} async-done(((bf16[256,512]{1,0:T(8,128)(2,1)}), bf16[8192,512]{1,0:T(8,128)(2,1)}) %all-gather.11.cloned.1.call-update) | async-done | bytes 8388624 | tf_op jit(solution)/shard_map/all_gather | solution.py:96
  215.7 7.0 %fusion.4 = f32[256,512]{1,0:T(8,128)S(1)} fusion(bf16[8192,512]{1,0:T(8,128)(2,1)} %all-gather.11.cloned.1.call-done, bf16[256,8192]{1,0:T(8,128)(2,1)} %param.15, f32[8192]{0:T(1024)S(1)} %copy-done.1, f32[256]{0:T(256)S(1)} %add_rsqrt_fusion), kind=kOutput, calls=%fused_computation.7 | convolution fusion | flops 2155872256 | bytes 13140992 | tf_op jit(solution)/shard_map/dot_general | solution.py:63
  223.5 1.5 collective-permute-start
  225.0 1.8 collective-permute-start.1
  226.8 11.9 %all_gather.23 = f32[32,512]{1,0:T(8,128)S(1)} all-gather(f32[8,512]{1,0:T(8,128)S(1)} %bitcast.84), channel_id=1, replica_groups=mesh['fsdp'=32,'seq'=4] {'seq'}, dimensions={0}, use_global_device_ids=true | all-gather | bytes 81920 | tf_op jit(solution)/shard_map/all_gather | solution.py:111
  239.5 4.7 %collective-permute-done.2 = f32[8,512]{1,0:T(8,128)S(1)} collective-permute-done((f32[8,512]{1,0:T(8,128)S(1)}, f32[8,512]{1,0:T(8,128)S(1)}, u32[]{:S(2)}, u32[]{:S(2)}) %collective-permute-start.2) | collective-permute-done | bytes 16416 | tf_op jit(solution)/shard_map/ppermute | solution.py:19
  244.2 0.8 fusion.16
  (35 shorter events, 3.8 us)
Async XLA Ops:
  7.2 5.5 %copy-start = (f32[4,4,128]{2,1,0:T(4,128)S(1)}, f32[4,4,128]{2,1,0:T(4,128)}, u32[]{:S(2)}) copy-start(f32[4,4,128]{2,1,0:T(4,128)} %param.19) | copy-start | bytes 24580
  7.2 51.8 %all-gather.5.cloned.1.call-start = ((), (), s32[]{:S(2)}) async-start(), calls=%async_computation | async-start | bytes 4325376 | tf_op jit(solution)/shard_map/all_gather | solution.py:84
  7.9 98.8 %all-gather.7.cloned.1.call-start = ((), (), s32[]{:S(2)}) async-start(), calls=%async_computation.1 | async-start | bytes 4325376 | tf_op jit(solution)/shard_map/all_gather | solution.py:85
  8.7 152.5 %all-gather.9.cloned.1.call-start = ((), (), s32[]{:S(2)}) async-start(), calls=%async_computation.2 | async-start | bytes 8650752 | tf_op jit(solution)/shard_map/all_gather | solution.py:95
  9.4 206.3 %all-gather.11.cloned.1.call-start = ((), (), s32[]{:S(2)}) async-start(), calls=%async_computation.3 | async-start | bytes 8650752 | tf_op jit(solution)/shard_map/all_gather | solution.py:96
  18.1 88.7 %copy-start.2 = (f32[1024]{0:T(1024)S(1)}, f32[1024]{0:T(1024)}, u32[]{:S(2)}) copy-start(f32[1024]{0:T(1024)} %param.14) | copy-start | bytes 12292
  69.0 92.2 %copy-start.1 = (f32[8192]{0:T(1024)S(1)}, f32[8192]{0:T(1024)}, u32[]{:S(2)}) copy-start(f32[8192]{0:T(1024)} %param.16) | copy-start | bytes 98308
  223.5 15.7 %collective-permute-start = (f32[8,512]{1,0:T(8,128)S(1)}, f32[8,512]{1,0:T(8,128)S(1)}, u32[]{:S(2)}, u32[]{:S(2)}) collective-permute-start(f32[8,512]{1,0:T(8,128)S(1)} %bitcast.85), channel_id=1, source_target_pairs={{0,1},{1,2},{2,3},{3,0},{4,5},{5,6},{6,7},{7,4},{8,9},{9,10},{10,1... | collective-permute-start | bytes 49160 | tf_op jit(solution)/shard_map/ppermute | solution.py:19
  225.0 14.5 %collective-permute-start.1 = (f32[8,512]{1,0:T(8,128)S(1)}, f32[8,512]{1,0:T(8,128)S(1)}, u32[]{:S(2)}, u32[]{:S(2)}) collective-permute-start(f32[8,512]{1,0:T(8,128)S(1)} %bitcast.86), channel_id=1, source_target_pairs={{0,3},{1,0},{2,1},{3,2},{4,7},{5,4},{6,5},{7,6},{8,11},{9,8},{10,9... | collective-permute-start | bytes 49160 | tf_op jit(solution)/shard_map/ppermute | solution.py:22
  239.2 5.0 %collective-permute-start.2 = (f32[8,512]{1,0:T(8,128)S(1)}, f32[8,512]{1,0:T(8,128)S(1)}, u32[]{:S(2)}, u32[]{:S(2)}) collective-permute-start(f32[8,512]{1,0:T(8,128)S(1)} %collective-permute-done), channel_id=1, source_target_pairs={{0,1},{1,2},{2,3},{3,0},{4,5},{5,6},{6,7},{7,4},{8,9},{9,10},{10,1... | collective-permute-start | bytes 49160 | tf_op jit(solution)/shard_map/ppermute | solution.py:19
Sparse Core Ops, SparseCore 0:
  10.2 48.6 all-gather.4
  61.2 45.4 all-gather.6
  109.0 52.1 all-gather.8
  163.3 52.3 all-gather.10
